TPU v7x, 256 devices: a whole 4x4x8 slice. The times are simulated.
256 devices in a mesh: seq: 128 (over z, y, x_lo, core), dp: 2 (over x_hi).
Axes of the slice: x: 4 (x_hi: 2, x_lo: 2; x = x_hi * 2 + x_lo), y: 4, z: 8, core: 2. Of those that a mesh axis runs over, the one named last changes fastest.
Arguments:
- frames: bfloat16 [2, 16384, 1024], P('dp', 'seq'), may hold values from -36 to 36
- kernel: bfloat16 [31, 1024], replicated, may hold values from -1 to 1
- norm_gain: float32 [1024], replicated, may hold values from 0.5 to 1.5
- router: bfloat16 [1024, 32], replicated, may hold values from -0.1875 to 0.1875
- experts: int32 [2, 16384, 2], P('dp', 'seq'), may hold values from 0 to 31, all different within a row; in each aligned block of 128 rows (0 to 127, 128 to 255, ..., all dimensions but the last counted through in order) at most 16 rows name the same one
- w_in: bfloat16 [128, 1024, 512], P('seq'), may hold values from -0.1875 to 0.1875
- w_out: bfloat16 [128, 512, 1024], P('seq'), may hold values from -0.125 to 0.125
- cotangent: bfloat16 [2, 16384, 1024], P('dp', 'seq'), may hold values from -8 to 8
Outputs:
- mixed: bfloat16 [2, 16384, 1024], P('dp', 'seq')
- grad_frames: bfloat16 [2, 16384, 1024], P('dp', 'seq')
- grad_kernel: float32 [31, 1024], replicated
- grad_gain: float32 [1024], replicated
- grad_router: float32 [1024, 32], replicated
- grad_w_in: float32 [128, 1024, 512], P('seq')
- grad_w_out: float32 [128, 512, 1024], P('seq')
Inputs may be any that keep to these rules, and one draw needn't show every extreme that they name: Each frame names 2 different experts; in each aligned block of 128 frames no expert is named more than 16 times, a bound that some block reaches.
All inputs are finite; a program needn't handle non-finite values.
Results may differ from a plain program's by a relative error of at most 0.0075.
Values may be sent and summed in bfloat16 or wider, within the bound.
No kernel may reach another device: no remote copies, remote signals or barrier semaphores. Data moves between devices by JAX's collectives and lax.ppermute only.
A program may use at most 128 MiB of HBM per device.

v0:
```python
import jax
import jax.numpy as jnp
from jax import lax
from jax.sharding import Mesh
from jax.sharding import PartitionSpec as P

eps = 1e-06

SEQ = ("z", "y", "xl", "c")
GRP = ("z", "y")


def padded_2(shard, axis, size, width):
    length = shard.shape[0]
    up = [(i, (i + 1) % size) for i in range(size - 1)]
    down = [(j, i) for i, j in up]
    last = lax.slice_in_dim(shard, length - width, length, axis=0)
    initial = lax.slice_in_dim(shard, 0, width, axis=0)
    before = lax.ppermute(last, axis, up)
    after = lax.ppermute(initial, axis, down)
    return jnp.concatenate([before, shard, after], axis=0)


def swap(value, axis):
    return lax.ppermute(value, axis, [(0, 1), (1, 0)])


def gather_slices(weights):
    pair = jnp.stack([weights, swap(weights, "xl")])
    return jnp.stack([pair, swap(pair, "c")])


def group_sum(value, axes, size):
    received = [value] + [
        lax.ppermute(value, axes, [(i, i ^ offset) for i in range(size)]) for offset in range(1, size)
    ]
    me = lax.axis_index(axes)
    stacked = jnp.stack(received)
    ordered = jnp.take(stacked, jnp.bitwise_xor(me, jnp.arange(size, dtype=me.dtype)), axis=0)
    total = ordered[0]
    for member in range(1, size):
        total = total + ordered[member]
    return total


def conv_forward(padded, kernel, row_count):
    summed = jnp.zeros((row_count, padded.shape[1]), jnp.float32)
    for offset in range(kernel.shape[0]):
        summed = summed + kernel[offset].astype(jnp.float32) * padded[
            offset : offset + row_count
        ].astype(jnp.float32)
    return summed


def conv_transpose(padded, kernel, row_count):
    length = kernel.shape[0]
    summed = jnp.zeros((row_count, padded.shape[1]), jnp.float32)
    for offset in range(length):
        start = length - 1 - offset
        summed = summed + kernel[offset].astype(jnp.float32) * padded[start : start + row_count]
    return summed


def kernel_terms(padded, upstream, length, row_count):
    return jnp.stack(
        [
            jnp.sum(padded[offset : offset + row_count].astype(jnp.float32) * upstream, axis=0)
            for offset in range(length)
        ]
    )


def normalize(summed, norm_gain):
    square = jnp.mean(summed * summed, axis=-1, keepdims=True)
    return summed * lax.rsqrt(square + eps) * norm_gain


def slot_numbers(expert_ids, expert_count):
    onehot = (expert_ids[:, None] == jnp.arange(expert_count, dtype=jnp.int32)[None, :]).astype(
        jnp.int32
    )
    ranks = jnp.cumsum(onehot, axis=0) - onehot
    return jnp.sum(ranks * onehot, axis=1)


def gate_values(normed_b, router, first_ids, second_ids):
    logits = jnp.dot(normed_b, router, preferred_element_type=jnp.float32)
    columns = jnp.arange(router.shape[1], dtype=jnp.int32)[None, :]
    pick_diff = (first_ids[:, None] == columns).astype(jnp.float32) - (
        second_ids[:, None] == columns
    ).astype(jnp.float32)
    gate_one = jax.nn.sigmoid(jnp.sum(logits * pick_diff, axis=1))
    return (gate_one, 1.0 - gate_one, pick_diff)


def swish_parts(pre_act):
    squash = jax.nn.sigmoid(pre_act)
    return (pre_act * squash, squash * (1.0 + pre_act * (1.0 - squash)))


def gate_backward(upstream, out_one, out_two, gate_one, gate_two, pick_diff, normed_b, router):
    grad_gap = (
        (jnp.sum(upstream * out_one, axis=1) - jnp.sum(upstream * out_two, axis=1))
        * gate_one
        * gate_two
    )
    grad_logits = (grad_gap[:, None] * pick_diff).astype(jnp.bfloat16)
    router_term = jnp.dot(normed_b.T, grad_logits, preferred_element_type=jnp.float32)
    normed_term = jnp.dot(grad_logits, router.T, preferred_element_type=jnp.float32)
    return (router_term, normed_term)


def body(frames, kernel, norm_gain, router, experts, w_in, w_out, cotangent):
    inputs_dev = frames[0]
    row_count = inputs_dev.shape[0]
    width = inputs_dev.shape[1]
    length = kernel.shape[0]
    half_width = length // 2
    expert_count = router.shape[1]
    top_count = experts.shape[2]
    capacity = 2 * row_count * top_count // expert_count
    seq_size = lax.psum(1, SEQ)
    in_weights = w_in[0]
    out_weights = w_out[0]
    padded = padded_2(inputs_dev, SEQ, seq_size, half_width)
    summed = inputs_dev.astype(jnp.float32) + conv_forward(padded, kernel, row_count)
    normed_b = normalize(summed, norm_gain).astype(jnp.bfloat16)
    choice_ids = experts[0]
    gate_one, gate_two, pick_diff = gate_values(
        normed_b, router, choice_ids[:, 0], choice_ids[:, 1]
    )
    flat_ids = choice_ids.reshape(-1)
    slot_index = slot_numbers(flat_ids, expert_count)
    position = flat_ids * capacity + slot_index
    dispatch_table = (
        lax.broadcasted_iota(jnp.int32, (expert_count * capacity, flat_ids.shape[0]), 0)
        == position[None, :]
    ).astype(jnp.bfloat16)

    upstream = cotangent[0].astype(jnp.float32)
    repeated = jnp.repeat(normed_b, top_count, axis=0)
    grad_assigned = jnp.stack([gate_one[:, None] * upstream, gate_two[:, None] * upstream], axis=1)
    grad_values = grad_assigned.reshape(row_count * top_count, width).astype(jnp.bfloat16)
    both = jnp.concatenate([repeated, grad_values], axis=1)
    packed = jnp.dot(dispatch_table, both, preferred_element_type=jnp.float32).astype(jnp.bfloat16)
    packed = packed.reshape(expert_count, capacity, 2 * width)
    arrived = lax.all_to_all(packed, GRP, split_axis=0, concat_axis=0, tiled=True)
    in_all = gather_slices(in_weights)
    out_all = gather_slices(out_weights)
    slices = in_all.shape[0] * in_all.shape[1]
    hid = in_weights.shape[1]
    in_all = in_all.reshape(slices, width, hid)
    out_all = out_all.reshape(slices, hid, width)
    flat = arrived.reshape(-1, 2 * width)
    flat_rows = flat[:, :width]
    flat_grads = flat[:, width:]
    n_rows = flat.shape[0]

    in_cat = jnp.transpose(in_all, (1, 0, 2)).reshape(width, slices * hid)
    out_cat = out_all.reshape(slices * hid, width)
    pre_act = jnp.dot(flat_rows, in_cat, preferred_element_type=jnp.float32)
    hidden_f, slope = swish_parts(pre_act)
    hidden = hidden_f.astype(jnp.bfloat16)
    hidden_s = hidden.reshape(n_rows, slices, hid)
    partial_rows = jnp.einsum(
        "rsh,shd->srd", hidden_s, out_all, preferred_element_type=jnp.float32
    ).astype(jnp.bfloat16)
    expert_rows = partial_rows[0].astype(jnp.float32)
    for member in range(1, slices):
        expert_rows = expert_rows + partial_rows[member].astype(jnp.float32)
    grad_hidden = jnp.dot(flat_grads, out_cat.T, preferred_element_type=jnp.float32)
    grad_pre = (grad_hidden * slope).astype(jnp.bfloat16)
    out_term = jnp.dot(hidden.T, flat_grads, preferred_element_type=jnp.float32)
    in_term = jnp.dot(flat_rows.T, grad_pre, preferred_element_type=jnp.float32)
    grad_parts = jnp.einsum(
        "rsh,sdh->srd", grad_pre.reshape(n_rows, slices, hid), in_all,
        preferred_element_type=jnp.float32,
    ).astype(jnp.bfloat16)
    grad_rows = grad_parts[0].astype(jnp.float32)
    for member in range(1, slices):
        grad_rows = grad_rows + grad_parts[member].astype(jnp.float32)

    in_term = jnp.transpose(in_term.reshape(width, slices, hid), (1, 0, 2))
    in_term = in_term.reshape(2, 2, width, hid)
    out_term = out_term.reshape(2, 2, width, hid)
    terms = jnp.concatenate([in_term, out_term], axis=3).astype(jnp.bfloat16)
    pair_terms = terms[0].astype(jnp.float32) + swap(terms[1], "c").astype(jnp.float32)
    own_terms = pair_terms[0] + swap(pair_terms[1].astype(jnp.bfloat16), "xl").astype(jnp.float32)
    mine = own_terms.astype(jnp.bfloat16)
    other = swap(mine, "dp")
    dp_first = lax.axis_index("dp") == 0
    first = jnp.where(dp_first, mine, other).astype(jnp.float32)
    second = jnp.where(dp_first, other, mine).astype(jnp.float32)
    grad_terms = first + second
    grad_in = grad_terms[:, :hid]
    grad_out = grad_terms[:, hid:].reshape(hid, width)

    back = jnp.concatenate([expert_rows, grad_rows], axis=1).astype(jnp.bfloat16)
    back = back.reshape(expert_count, capacity, 2 * width)
    totals = lax.all_to_all(back, GRP, split_axis=0, concat_axis=0, tiled=True)
    totals = totals.reshape(expert_count * capacity, 2 * width)
    picked = jnp.take(totals, position, axis=0).astype(jnp.float32)
    picked = picked.reshape(row_count, top_count, 2 * width)
    out_one = picked[:, 0, :width]
    out_two = picked[:, 1, :width]
    normed_grads = picked[:, 0, width:] + picked[:, 1, width:]

    mixed = (summed + gate_one[:, None] * out_one + gate_two[:, None] * out_two).astype(
        jnp.bfloat16
    )
    router_term, normed_term = gate_backward(
        upstream, out_one, out_two, gate_one, gate_two, pick_diff, normed_b, router
    )
    pullback = jax.vjp(normalize, summed, norm_gain)[1]
    summed_grad, gain_term = pullback(normed_grads + normed_term)
    upstream_total = upstream + summed_grad
    padded_grad = padded_2(
        upstream_total.astype(jnp.bfloat16), SEQ, seq_size, half_width
    ).astype(upstream_total.dtype)
    grad_frames = (upstream_total + conv_transpose(padded_grad, kernel, row_count)).astype(
        jnp.bfloat16
    )
    kernel_term = kernel_terms(padded, upstream_total, length, row_count)
    small = jnp.concatenate([kernel_term, gain_term[None, :], router_term.T], axis=0)
    local = ("xl", "c", "dp")
    chunks = small.reshape(8, small.shape[0] // 8, small.shape[1])
    me = lax.axis_index(local)
    chunk = lax.dynamic_index_in_dim(chunks, me, axis=0, keepdims=False)
    for offset in range(1, 8):
        piece = lax.dynamic_index_in_dim(chunks, jnp.bitwise_xor(me, offset), axis=0, keepdims=False)
        chunk = chunk + lax.ppermute(piece, local, [(i, i ^ offset) for i in range(8)])
    chunk = group_sum(chunk, "y", 4)
    for bit in (1, 2, 4):
        chunk = chunk + lax.ppermute(chunk, "z", [(i, i ^ bit) for i in range(8)])
    gathered = [chunk] + [
        lax.ppermute(chunk, local, [(i, i ^ offset) for i in range(8)]) for offset in range(1, 8)
    ]
    small = jnp.take(jnp.stack(gathered), jnp.bitwise_xor(me, jnp.arange(8, dtype=me.dtype)), axis=0)
    small = small.reshape(chunks.shape[0] * chunks.shape[1], chunks.shape[2])
    grad_kernel = small[:length]
    grad_gain = small[length]
    grad_router = small[length + 1 :].T
    return (
        mixed[None],
        grad_frames[None],
        grad_kernel,
        grad_gain,
        grad_router,
        grad_in[None],
        grad_out[None],
    )


def solution(mesh):
    split_mesh = Mesh(mesh.devices.reshape(8, 4, 2, 2, 2), SEQ + ("dp",))
    return jax.shard_map(
        body,
        mesh=split_mesh,
        in_specs=(
            P("dp", SEQ, None),
            P(),
            P(),
            P(),
            P("dp", SEQ, None),
            P(SEQ, None, None),
            P(SEQ, None, None),
            P("dp", SEQ, None),
        ),
        out_specs=(
            P("dp", SEQ, None),
            P("dp", SEQ, None),
            P(),
            P(),
            P(),
            P(SEQ, None, None),
            P(SEQ, None, None),
        ),
        check_vma=False,
    )
```

profile of v0, /device:TPU:1, one launch (start us, length us, event | category | flops | bytes accessed | tf_op | source)
XLA Modules:
  0.0 352.6 jit_solution(10478027681864325833)
XLA Ops:
  0.6 0.8 slice_bitcast_fusion.5
  1.5 5.1 %collective-permute-start.1 = (bf16[15,1024]{1,0:T(8,128)(2,1)S(1)}, bf16[15,1024]{1,0:T(8,128)(2,1)S(1)}, u32[]{:S(2)}, u32[]{:S(2)}) collective-permute-start(bf16[15,1024]{1,0:T(8,128)(2,1)S(1)} %get-tuple-element.69), channel_id=1, source_target_pairs={{2,0},{4,2},{6,4},{8,6},{10,8},{12,10},{14,12},{16,14},{18,16},{20... | collective-permute-start | bytes 92168 | tf_op jit(solution)/shard_map/ppermute | solution.py:20
  6.6 1.9 collective-permute-start
  8.5 1.1 slice_convert_fusion.30
  9.6 1.2 slice_convert_fusion.31
  13.6 10.6 %multiply_reduce_fusion.2 = (f32[128]{0:T(128)S(1)}, f32[128,1024]{1,0:T(8,128)S(1)}) fusion(bf16[15,1024]{1,0:T(8,128)(2,1)S(1)} %collective-permute-done.1, bf16[128,1024]{1,0:T(8,128)(2,1)} %bitcast.271, f32[1024]{0:T(1024)S(1)} %bitcast.309, f32[1024]{0:T(1024)S(1)} %bitcast.311, f32[1024]{0:T(1024)S(1)} %bitcast.315, f32[1024]{0:T(1024)S(1)} %bitcast.317, ...), kind=kLoop, calls=%fused_computation.286 | loop fusion | flops 24248192 | bytes 975360 | tf_op jit(solution)/shard_map/reduce_sum | solution.py:74
  24.2 0.8 multiply_convert_fusion.2
  25.2 1.1 fusion.85
  27.6 2.0 convolution_convert_fusion.2
  29.7 10.9 %all-to-all-start = ((bf16[32,16,2048]{2,1,0:T(8,128)(2,1)}), bf16[32,16,2048]{2,1,0:T(8,128)(2,1)}, u32[]{:S(2)}, u32[]{:S(2)}) async-start(bf16[32,16,2048]{2,1,0:T(8,128)(2,1)} %bitcast.39), calls=%async_computation | async-start | bytes 4194304 | tf_op jit(solution)/shard_map/all_to_all | solution.py:147
  40.6 4.1 %collective-permute-start.2 = (bf16[1024,512]{1,0:T(8,128)(2,1)S(1)}, bf16[1024,512]{1,0:T(8,128)(2,1)S(1)}, u32[]{:S(2)}, u32[]{:S(2)}) collective-permute-start(bf16[1024,512]{1,0:T(8,128)(2,1)S(1)} %bitcast.284), channel_id=1, source_target_pairs={{0,4},{4,0},{1,5},{5,1},{2,6},{6,2},{3,7},{7,3},{8,12},{12,8},{9,1... | collective-permute-start | bytes 3145736 | tf_op jit(solution)/shard_map/ppermute | solution.py:25
  44.8 23.7 %collective-permute-done.2 = bf16[1024,512]{1,0:T(8,128)(2,1)S(1)} collective-permute-done((bf16[1024,512]{1,0:T(8,128)(2,1)S(1)}, bf16[1024,512]{1,0:T(8,128)(2,1)S(1)}, u32[]{:S(2)}, u32[]{:S(2)}) %collective-permute-start.2) | collective-permute-done | bytes 1048608 | tf_op jit(solution)/shard_map/ppermute | solution.py:25
  68.9 21.9 %collective-permute-done.4 = bf16[512,1024]{1,0:T(8,128)(2,1)S(1)} collective-permute-done((bf16[512,1024]{1,0:T(8,128)(2,1)S(1)}, bf16[512,1024]{1,0:T(8,128)(2,1)S(1)}, u32[]{:S(2)}, u32[]{:S(2)}) %collective-permute-start.4) | collective-permute-done | bytes 1048608 | tf_op jit(solution)/shard_map/ppermute | solution.py:25
  90.8 1.6 fusion.177
  92.9 2.3 pad_maximum_fusion.1
  95.2 6.3 %copy.47 = bf16[1024,4,512]{0,2,1:T(8,128)(2,1)} copy(bf16[1024,4,512]{2,0,1:T(8,128)(2,1)} %bitcast.268) | data formatting | bytes 8388608 | tf_op jit(solution)/shard_map/transpose | solution.py:159
  101.5 3.9 %pad_maximum_fusion.2 = bf16[2,2,512,1024]{3,2,1,0:T(8,128)(2,1)} fusion(bf16[1,2,512,1024]{3,2,1,0:T(8,128)(2,1)} %bitcast.51, bf16[1,2,512,1024]{3,2,1,0:T(8,128)(2,1)S(1)} %get-tuple-element.52), kind=kLoop, calls=%fused_computation.15 | loop fusion | flops 2097152 | bytes 8388608 | tf_op jit(solution)/shard_map/stack | solution.py:30
  105.5 5.5 %multiply_convert_fusion.1 = (bf16[512,2048]{1,0:T(8,128)(2,1)S(1)}, f32[512,2048]{1,0:T(8,128)S(1)}) fusion(bf16[1024,2048]{0,1:T(8,128)(2,1)} %bitcast.278, bf16[512,2048]{1,0:T(8,128)(2,1)} %bitcast.40), kind=kOutput, calls=%fused_computation.18 | convolution fusion | flops 2152726528 | bytes 11534336 | tf_op jit(solution)/shard_map/dot_general | solution.py:161
  111.0 5.0 %multiply_convert_fusion = bf16[512,2048]{1,0:T(8,128)(2,1)S(1)} fusion(f32[512,2048]{1,0:T(8,128)S(1)} %get-tuple-element.104, bf16[2048,1024]{1,0:T(8,128)(2,1)S(1)} %bitcast.276, bf16[512,2048]{1,0:T(8,128)(2,1)} %bitcast.40), kind=kOutput, calls=%fused_computation.17 | convolution fusion | flops 2156920832 | bytes 11534336 | tf_op jit(solution)/shard_map/dot_general | solution.py:171
  116.0 2.4 convolution_convert_fusion.3
  118.4 0.9 add_convert_fusion
  119.3 2.3 convolution_convert_fusion.4
  121.6 0.9 add_convert_fusion.1
  122.5 1.5 pad_maximum_fusion.5
  124.0 9.7 %all-to-all-start.1 = ((bf16[32,16,2048]{2,1,0:T(8,128)(2,1)}), bf16[32,16,2048]{2,1,0:T(8,128)(2,1)S(1)}, u32[]{:S(2)}, u32[]{:S(2)}) async-start(bf16[32,16,2048]{2,1,0:T(8,128)(2,1)} %pad_maximum_fusion.5), calls=%async_computation.1 | async-start | bytes 4194304 | tf_op jit(solution)/shard_map/all_to_all | solution.py:200
  133.7 6.2 %convolution_convert_fusion = bf16[2048,1024]{1,0:T(8,128)(2,1)} fusion(bf16[512,2048]{1,0:T(8,128)(2,1)} %copy-done.15, bf16[512,2048]{1,0:T(8,128)(2,1)} %bitcast.40), kind=kOutput, calls=%fused_computation.20 | convolution fusion | flops 2149580800 | bytes 7340032 | tf_op jit(solution)/shard_map/dot_general | solution.py:173
  139.9 7.1 %reshape.322 = bf16[2,2,1024,512]{3,2,1,0:T(8,128)(2,1)} reshape(bf16[2048,1024]{1,0:T(8,128)(2,1)} %convolution_convert_fusion) | data formatting | bytes 8388608 | tf_op jit(solution)/shard_map/reshape | solution.py:185
  147.0 6.3 %convolution_convert_fusion.1 = bf16[1024,2048]{1,0:T(8,128)(2,1)} fusion(bf16[512,2048]{1,0:T(8,128)(2,1)} %copy-done.14, bf16[512,2048]{1,0:T(8,128)(2,1)} %bitcast.40), kind=kOutput, calls=%fused_computation.21 | convolution fusion | flops 2149580800 | bytes 7340032 | tf_op jit(solution)/shard_map/dot_general | solution.py:174
  153.3 7.9 %reshape.320 = bf16[1024,4,512]{2,1,0:T(4,128)(2,1)} reshape(bf16[1024,2048]{1,0:T(8,128)(2,1)} %convolution_convert_fusion.1) | data formatting | bytes 8388608 | tf_op jit(solution)/shard_map/reshape | solution.py:183
  161.2 3.2 copy.52
  164.7 3.0 fusion.4
  168.7 13.7 %all-to-all-done.1 = bf16[32,16,2048]{2,1,0:T(8,128)(2,1)S(1)} async-done(((bf16[32,16,2048]{2,1,0:T(8,128)(2,1)}), bf16[32,16,2048]{2,1,0:T(8,128)(2,1)S(1)}, u32[]{:S(2)}, u32[]{:S(2)}) %all-to-all-start.1) | async-done | bytes 2097184 | tf_op jit(solution)/shard_map/all_to_all | solution.py:200
  182.4 2.3 gather_fusion
  184.8 1.8 gather.17
  187.3 1.0 fusion.88
  188.9 0.8 fusion.84
  191.7 4.2 %convert_add_fusion = f32[2,1024,1024]{2,1,0:T(8,128)S(1)} fusion(bf16[2,1024,1024]{2,1,0:T(8,128)(2,1)} %collective-permute-done.28, bf16[2,2,1024,512]{3,2,1,0:T(8,128)(2,1)} %bitcast.267, bf16[2,2,1024,512]{3,2,1,0:T(8,128)(2,1)} %reshape.322), kind=kLoop, calls=%fused_computation.5 | loop fusion | flops 14680064 | bytes 20971520 | tf_op jit(solution)/shard_map/add | solution.py:187
  196.0 3.2 copy-done.3
  199.7 5.3 %collective-permute-start.14 = (f32[8,1024]{1,0:T(8,128)S(1)}, f32[8,1024]{1,0:T(8,128)S(1)}, u32[]{:S(2)}, u32[]{:S(2)}) collective-permute-start(f32[8,1024]{1,0:T(8,128)S(1)} %get-tuple-element.58), channel_id=1, source_target_pairs={{0,7},{1,6},{2,5},{3,4},{4,3},{5,2},{6,1},{7,0},{8,15},{9,14},{10,... | collective-permute-start | bytes 98312 | tf_op jit(solution)/shard_map/ppermute | solution.py:231
  205.0 1.0 collective-permute-start.11
  206.6 2.3 collective-permute-start.10
  208.9 39.5 %collective-permute-done.13 = f32[8,1024]{1,0:T(8,128)S(1)} collective-permute-done((f32[8,1024]{1,0:T(8,128)S(1)}, f32[8,1024]{1,0:T(8,128)S(1)}, u32[]{:S(2)}, u32[]{:S(2)}) %collective-permute-start.13) | collective-permute-done | bytes 32800 | tf_op jit(solution)/shard_map/ppermute | solution.py:231
  248.4 2.5 collective-permute-start.8
  251.0 1.9 collective-permute-done.8
  252.9 0.8 fusion.164
  253.7 4.1 %collective-permute-start.17 = (f32[8,1024]{1,0:T(8,128)S(1)}, f32[8,1024]{1,0:T(8,128)S(1)}, u32[]{:S(2)}, u32[]{:S(2)}) collective-permute-start(f32[8,1024]{1,0:T(8,128)S(1)} %fusion.164), channel_id=1, source_target_pairs={{0,24},{8,16},{16,8},{24,0},{1,25},{9,17},{17,9},{25,1},{2,26},{10... | collective-permute-start | bytes 98312 | tf_op jit(solution)/shard_map/ppermute | solution.py:35
  259.2 3.2 collective-permute-done.16
  263.1 1.7 collective-permute-start.18
  264.7 5.2 %collective-permute-start.7 = (bf16[15,1024]{1,0:T(8,128)(2,1)S(1)}, bf16[15,1024]{1,0:T(8,128)(2,1)S(1)}, u32[]{:S(2)}, u32[]{:S(2)}) collective-permute-start(bf16[15,1024]{1,0:T(8,128)(2,1)S(1)} %get-tuple-element.65), channel_id=1, source_target_pairs={{2,0},{4,2},{6,4},{8,6},{10,8},{12,10},{14,12},{16,14},{18,16},{20... | collective-permute-start | bytes 92168 | tf_op jit(solution)/shard_map/ppermute | solution.py:20
  269.9 1.9 collective-permute-start.6
  272.3 3.4 collective-permute-done.19
  275.8 6.7 %collective-permute-done.20 = f32[8,1024]{1,0:T(8,128)S(1)} collective-permute-done((f32[8,1024]{1,0:T(8,128)S(1)}, f32[8,1024]{1,0:T(8,128)S(1)}, u32[]{:S(2)}, u32[]{:S(2)}) %collective-permute-start.20) | collective-permute-done | bytes 32800 | tf_op jit(solution)/shard_map/ppermute | solution.py:234
  282.4 2.4 collective-permute-start.21
  284.8 3.6 %fusion.3 = bf16[1024,1024]{1,0:T(8,128)(2,1)S(1)} fusion(f32[2,1024,1024]{2,1,0:T(8,128)} %copy-done.3, bf16[1024,1024]{1,0:T(8,128)(2,1)} %collective-permute-done.29), kind=kLoop, calls=%fused_computation.11 | loop fusion | flops 3145728 | bytes 8388608 | tf_op jit(solution)/shard_map/convert_element_type | solution.py:189
  289.2 2.7 fusion.153
  291.9 3.4 collective-permute-start.22
  295.3 2.0 collective-permute-start.23
  297.3 1.2 collective-permute-start.25
  298.5 1.1 collective-permute-start.26
  299.6 39.3 %collective-permute-done.23 = f32[8,1024]{1,0:T(8,128)S(1)} collective-permute-done((f32[8,1024]{1,0:T(8,128)S(1)}, f32[8,1024]{1,0:T(8,128)S(1)}, u32[]{:S(2)}, u32[]{:S(2)}) %collective-permute-start.23) | collective-permute-done | bytes 32800 | tf_op jit(solution)/shard_map/ppermute | solution.py:236
  339.0 4.5 %collective-permute-done.27 = f32[8,1024]{1,0:T(8,128)S(1)} collective-permute-done((f32[8,1024]{1,0:T(8,128)S(1)}, f32[8,1024]{1,0:T(8,128)S(1)}, u32[]{:S(2)}, u32[]{:S(2)}) %collective-permute-start.27) | collective-permute-done | bytes 32800 | tf_op jit(solution)/shard_map/ppermute | solution.py:236
  346.1 2.5 convert_add_fusion.1
  348.7 1.9 fusion.180
  350.5 1.7 broadcast_in_dim_reshape.3
  (138 shorter events, 16.8 us)
Async XLA Ops:
  0.6 24.3 %copy-start = (bf16[1024,32]{0,1:T(8,128)(2,1)S(1)}, bf16[1024,32]{0,1:T(8,128)(2,1)}, u32[]{:S(2)}) copy-start(bf16[1024,32]{0,1:T(8,128)(2,1)} %param.11) | copy-start | bytes 196612
  1.5 12.1 %collective-permute-start.1 = (bf16[15,1024]{1,0:T(8,128)(2,1)S(1)}, bf16[15,1024]{1,0:T(8,128)(2,1)S(1)}, u32[]{:S(2)}, u32[]{:S(2)}) collective-permute-start(bf16[15,1024]{1,0:T(8,128)(2,1)S(1)} %get-tuple-element.69), channel_id=1, source_target_pairs={{2,0},{4,2},{6,4},{8,6},{10,8},{12,10},{14,12},{16,14},{18,16},{20... | collective-permute-start | bytes 92168 | tf_op jit(solution)/shard_map/ppermute | solution.py:20
  6.6 7.0 %collective-permute-start = (bf16[15,1024]{1,0:T(8,128)(2,1)S(1)}, bf16[15,1024]{1,0:T(8,128)(2,1)S(1)}, u32[]{:S(2)}, u32[]{:S(2)}) collective-permute-start(bf16[15,1024]{1,0:T(8,128)(2,1)S(1)} %get-tuple-element.68), channel_id=1, source_target_pairs={{0,2},{2,4},{4,6},{6,8},{8,10},{10,12},{12,14},{14,16},{16,18},{18... | collective-permute-start | bytes 92168 | tf_op jit(solution)/shard_map/ppermute | solution.py:19
  29.7 10.9 %copy-start.8 = (bf16[1,1024,512]{2,1,0:T(8,128)(2,1)S(1)}, bf16[1,1024,512]{2,1,0:T(8,128)(2,1)}, u32[]{:S(2)}) copy-start(bf16[1,1024,512]{2,1,0:T(8,128)(2,1)} %param.13) | copy-start | bytes 3145732
  29.7 15.0 %copy-start.9 = (bf16[1,512,1024]{2,1,0:T(8,128)(2,1)S(1)}, bf16[1,512,1024]{2,1,0:T(8,128)(2,1)}, u32[]{:S(2)}) copy-start(bf16[1,512,1024]{2,1,0:T(8,128)(2,1)} %param.14) | copy-start | bytes 3145732
  29.7 75.8 %all-to-all-start = ((bf16[32,16,2048]{2,1,0:T(8,128)(2,1)}), bf16[32,16,2048]{2,1,0:T(8,128)(2,1)}, u32[]{:S(2)}, u32[]{:S(2)}) async-start(bf16[32,16,2048]{2,1,0:T(8,128)(2,1)} %bitcast.39), calls=%async_computation | async-start | bytes 4194304 | tf_op jit(solution)/shard_map/all_to_all | solution.py:147
  40.5 50.2 %copy-start.10 = (bf16[1,512,1024]{2,1,0:T(8,128)(2,1)S(1)}, bf16[1,512,1024]{2,1,0:T(8,128)(2,1)}, u32[]{:S(2)}) copy-start(bf16[1,512,1024]{2,1,0:T(8,128)(2,1)} %param.14) | copy-start | bytes 3145732
  40.6 27.9 %collective-permute-start.2 = (bf16[1024,512]{1,0:T(8,128)(2,1)S(1)}, bf16[1024,512]{1,0:T(8,128)(2,1)S(1)}, u32[]{:S(2)}, u32[]{:S(2)}) collective-permute-start(bf16[1024,512]{1,0:T(8,128)(2,1)S(1)} %bitcast.284), channel_id=1, source_target_pairs={{0,4},{4,0},{1,5},{5,1},{2,6},{6,2},{3,7},{7,3},{8,12},{12,8},{9,1... | collective-permute-start | bytes 3145736 | tf_op jit(solution)/shard_map/ppermute | solution.py:25
  44.7 46.1 %collective-permute-start.4 = (bf16[512,1024]{1,0:T(8,128)(2,1)S(1)}, bf16[512,1024]{1,0:T(8,128)(2,1)S(1)}, u32[]{:S(2)}, u32[]{:S(2)}) collective-permute-start(bf16[512,1024]{1,0:T(8,128)(2,1)S(1)} %bitcast.285), channel_id=1, source_target_pairs={{0,4},{4,0},{1,5},{5,1},{2,6},{6,2},{3,7},{7,3},{8,12},{12,8},{9,1... | collective-permute-start | bytes 3145736 | tf_op jit(solution)/shard_map/ppermute | solution.py:25
  68.8 24.2 %collective-permute-start.3 = (bf16[2,1024,512]{2,1,0:T(8,128)(2,1)S(1)}, bf16[2,1024,512]{2,1,0:T(8,128)(2,1)S(1)}, u32[]{:S(2)}, u32[]{:S(2)}) collective-permute-start(bf16[2,1024,512]{2,1,0:T(8,128)(2,1)S(1)} %get-tuple-element.55), channel_id=1, source_target_pairs={{0,2},{2,0},{1,3},{3,1},{4,6},{6,4},{5,7},{7,5},{8,10},{10,8},{9,1... | collective-permute-start | bytes 6291464 | tf_op jit(solution)/shard_map/ppermute | solution.py:25
  92.4 9.1 %collective-permute-start.5 = (bf16[2,512,1024]{2,1,0:T(8,128)(2,1)}, bf16[2,512,1024]{2,1,0:T(8,128)(2,1)}, u32[]{:S(2)}, u32[]{:S(2)}) collective-permute-start(bf16[2,512,1024]{2,1,0:T(8,128)(2,1)} %get-tuple-element.53), channel_id=1, source_target_pairs={{0,2},{2,0},{1,3},{3,1},{4,6},{6,4},{5,7},{7,5},{8,10},{10,8},{9,1... | collective-permute-start | bytes 6291464 | tf_op jit(solution)/shard_map/ppermute | solution.py:25
  105.5 5.5 %copy-start.6 = (bf16[2,2,512,1024]{3,2,1,0:T(8,128)(2,1)S(1)}, bf16[2,2,512,1024]{3,2,1,0:T(8,128)(2,1)}, u32[]{:S(2)}) copy-start(bf16[2,2,512,1024]{3,2,1,0:T(8,128)(2,1)} %pad_maximum_fusion.2) | copy-start | bytes 12582916
  110.9 8.3 %copy-start.15 = (bf16[512,2048]{1,0:T(8,128)(2,1)}, bf16[512,2048]{1,0:T(8,128)(2,1)S(1)}, u32[]{:S(2)}) copy-start(bf16[512,2048]{1,0:T(8,128)(2,1)S(1)} %get-tuple-element.103) | copy-start | bytes 6291460
  110.9 5.0 %copy-start.4 = (bf16[2,2,1024,512]{3,2,1,0:T(8,128)(2,1)S(1)}, bf16[2,2,1024,512]{3,2,1,0:T(8,128)(2,1)}, u32[]{:S(2)}) copy-start(bf16[2,2,1024,512]{3,2,1,0:T(8,128)(2,1)} %pad_maximum_fusion.1) | copy-start | bytes 12582916
  115.9 2.4 copy-start.14
  124.0 58.4 %all-to-all-start.1 = ((bf16[32,16,2048]{2,1,0:T(8,128)(2,1)}), bf16[32,16,2048]{2,1,0:T(8,128)(2,1)S(1)}, u32[]{:S(2)}, u32[]{:S(2)}) async-start(bf16[32,16,2048]{2,1,0:T(8,128)(2,1)} %pad_maximum_fusion.5), calls=%async_computation.1 | async-start | bytes 4194304 | tf_op jit(solution)/shard_map/all_to_all | solution.py:200
  161.2 3.4 copy-start.1
  164.4 3.2 copy-start.2
  164.7 3.6 %copy-start.13 = (s32[1,128,2]{1,2,0:T(2,128)S(1)}, s32[1,128,2]{1,2,0:T(2,128)}, u32[]{:S(2)}) copy-start(s32[1,128,2]{1,2,0:T(2,128)} %param.12) | copy-start | bytes 3076
  167.6 24.1 %collective-permute-start.28 = (bf16[2,1024,1024]{2,1,0:T(8,128)(2,1)}, bf16[2,1024,1024]{2,1,0:T(8,128)(2,1)}, u32[]{:S(2)}, u32[]{:S(2)}) collective-permute-start(bf16[2,1024,1024]{2,1,0:T(8,128)(2,1)} %fusion.4), channel_id=1, source_target_pairs={{0,2},{2,0},{1,3},{3,1},{4,6},{6,4},{5,7},{7,5},{8,10},{10,8},{9,1... | collective-permute-start | bytes 12582920 | tf_op jit(solution)/shard_map/ppermute | solution.py:25
  184.8 2.5 copy-start.7
  184.8 3.5 %copy-start.11 = (f32[1024]{0:T(1024)S(1)}, f32[1024]{0:T(1024)}, u32[]{:S(2)}) copy-start(f32[1024]{0:T(1024)} %param.10) | copy-start | bytes 12292
  184.8 4.1 %copy-start.5 = (bf16[1,128,1024]{2,1,0:T(8,128)(2,1)S(1)}, bf16[1,128,1024]{2,1,0:T(8,128)(2,1)}, u32[]{:S(2)}) copy-start(bf16[1,128,1024]{2,1,0:T(8,128)(2,1)} %param.8) | copy-start | bytes 786436
  196.0 3.2 copy-start.3
  199.5 85.3 %collective-permute-start.29 = (bf16[1024,1024]{1,0:T(8,128)(2,1)S(1)}, bf16[1024,1024]{1,0:T(8,128)(2,1)}, u32[]{:S(2)}, u32[]{:S(2)}) collective-permute-start(bf16[1024,1024]{1,0:T(8,128)(2,1)S(1)} %fusion.5), channel_id=1, source_target_pairs={{0,4},{4,0},{1,5},{5,1},{2,6},{6,2},{3,7},{7,3},{8,12},{12,8},{9,1... | collective-permute-start | bytes 6291464 | tf_op jit(solution)/shard_map/ppermute | solution.py:25
  199.7 6.9 %collective-permute-start.14 = (f32[8,1024]{1,0:T(8,128)S(1)}, f32[8,1024]{1,0:T(8,128)S(1)}, u32[]{:S(2)}, u32[]{:S(2)}) collective-permute-start(f32[8,1024]{1,0:T(8,128)S(1)} %get-tuple-element.58), channel_id=1, source_target_pairs={{0,7},{1,6},{2,5},{3,4},{4,3},{5,2},{6,1},{7,0},{8,15},{9,14},{10,... | collective-permute-start | bytes 98312 | tf_op jit(solution)/shard_map/ppermute | solution.py:231
  205.0 43.4 %collective-permute-start.13 = (f32[8,1024]{1,0:T(8,128)S(1)}, f32[8,1024]{1,0:T(8,128)S(1)}, u32[]{:S(2)}, u32[]{:S(2)}) collective-permute-start(f32[8,1024]{1,0:T(8,128)S(1)} %get-tuple-element.59), channel_id=1, source_target_pairs={{0,6},{1,7},{2,4},{3,5},{4,2},{5,3},{6,0},{7,1},{8,14},{9,15},{10,... | collective-permute-start | bytes 98312 | tf_op jit(solution)/shard_map/ppermute | solution.py:231
  205.0 43.4 %collective-permute-start.12 = (f32[8,1024]{1,0:T(8,128)S(1)}, f32[8,1024]{1,0:T(8,128)S(1)}, u32[]{:S(2)}, u32[]{:S(2)}) collective-permute-start(f32[8,1024]{1,0:T(8,128)S(1)} %get-tuple-element.60), channel_id=1, source_target_pairs={{0,5},{1,4},{2,7},{3,6},{4,1},{5,0},{6,3},{7,2},{8,13},{9,12},{10,... | collective-permute-start | bytes 98312 | tf_op jit(solution)/shard_map/ppermute | solution.py:231
  205.0 46.0 %collective-permute-start.11 = (f32[8,1024]{1,0:T(8,128)S(1)}, f32[8,1024]{1,0:T(8,128)}, u32[]{:S(2)}, u32[]{:S(2)}) collective-permute-start(f32[8,1024]{1,0:T(8,128)S(1)} %get-tuple-element.61), channel_id=1, source_target_pairs={{0,4},{1,5},{2,6},{3,7},{4,0},{5,1},{6,2},{7,3},{8,12},{9,13},{10,... | collective-permute-start | bytes 98312 | tf_op jit(solution)/shard_map/ppermute | solution.py:231
  206.6 44.4 %collective-permute-start.10 = (f32[8,1024]{1,0:T(8,128)S(1)}, f32[8,1024]{1,0:T(8,128)}, u32[]{:S(2)}, u32[]{:S(2)}) collective-permute-start(f32[8,1024]{1,0:T(8,128)S(1)} %get-tuple-element.62), channel_id=1, source_target_pairs={{0,3},{1,2},{2,1},{3,0},{4,7},{5,6},{6,5},{7,4},{8,11},{9,10},{10,... | collective-permute-start | bytes 98312 | tf_op jit(solution)/shard_map/ppermute | solution.py:231
  248.4 2.6 collective-permute-start.9
  248.4 2.5 copy-start.12
  248.4 4.5 %collective-permute-start.8 = (f32[8,1024]{1,0:T(8,128)S(1)}, f32[8,1024]{1,0:T(8,128)}, u32[]{:S(2)}, u32[]{:S(2)}) collective-permute-start(f32[8,1024]{1,0:T(8,128)S(1)} %get-tuple-element.57), channel_id=1, source_target_pairs={{0,1},{1,0},{2,3},{3,2},{4,5},{5,4},{6,7},{7,6},{8,9},{9,8},{10,11... | collective-permute-start | bytes 98312 | tf_op jit(solution)/shard_map/ppermute | solution.py:231
  253.7 5.4 %collective-permute-start.17 = (f32[8,1024]{1,0:T(8,128)S(1)}, f32[8,1024]{1,0:T(8,128)S(1)}, u32[]{:S(2)}, u32[]{:S(2)}) collective-permute-start(f32[8,1024]{1,0:T(8,128)S(1)} %fusion.164), channel_id=1, source_target_pairs={{0,24},{8,16},{16,8},{24,0},{1,25},{9,17},{17,9},{25,1},{2,26},{10... | collective-permute-start | bytes 98312 | tf_op jit(solution)/shard_map/ppermute | solution.py:35
  257.9 4.5 %collective-permute-start.16 = (f32[8,1024]{1,0:T(8,128)S(1)}, f32[8,1024]{1,0:T(8,128)S(1)}, u32[]{:S(2)}, u32[]{:S(2)}) collective-permute-start(f32[8,1024]{1,0:T(8,128)S(1)} %fusion.164), channel_id=1, source_target_pairs={{0,16},{8,24},{16,0},{24,8},{1,17},{9,25},{17,1},{25,9},{2,18},{10... | collective-permute-start | bytes 98312 | tf_op jit(solution)/shard_map/ppermute | solution.py:35
  258.7 3.7 %collective-permute-start.15 = (f32[8,1024]{1,0:T(8,128)S(1)}, f32[8,1024]{1,0:T(8,128)S(1)}, u32[]{:S(2)}, u32[]{:S(2)}) collective-permute-start(f32[8,1024]{1,0:T(8,128)S(1)} %fusion.164), channel_id=1, source_target_pairs={{0,8},{8,0},{16,24},{24,16},{1,9},{9,1},{17,25},{25,17},{2,10},{10... | collective-permute-start | bytes 98312 | tf_op jit(solution)/shard_map/ppermute | solution.py:35
  263.1 8.8 %collective-permute-start.18 = (f32[8,1024]{1,0:T(8,128)S(1)}, f32[8,1024]{1,0:T(8,128)S(1)}, u32[]{:S(2)}, u32[]{:S(2)}) collective-permute-start(f32[8,1024]{1,0:T(8,128)S(1)} %fusion.158), channel_id=1, source_target_pairs={{0,32},{32,0},{64,96},{96,64},{128,160},{160,128},{192,224},{224,1... | collective-permute-start | bytes 98312 | tf_op jit(solution)/shard_map/ppermute | solution.py:234
  264.7 10.9 %collective-permute-start.7 = (bf16[15,1024]{1,0:T(8,128)(2,1)S(1)}, bf16[15,1024]{1,0:T(8,128)(2,1)S(1)}, u32[]{:S(2)}, u32[]{:S(2)}) collective-permute-start(bf16[15,1024]{1,0:T(8,128)(2,1)S(1)} %get-tuple-element.65), channel_id=1, source_target_pairs={{2,0},{4,2},{6,4},{8,6},{10,8},{12,10},{14,12},{16,14},{18,16},{20... | collective-permute-start | bytes 92168 | tf_op jit(solution)/shard_map/ppermute | solution.py:20
  269.9 5.7 %collective-permute-start.6 = (bf16[15,1024]{1,0:T(8,128)(2,1)S(1)}, bf16[15,1024]{1,0:T(8,128)(2,1)S(1)}, u32[]{:S(2)}, u32[]{:S(2)}) collective-permute-start(bf16[15,1024]{1,0:T(8,128)(2,1)S(1)} %get-tuple-element.64), channel_id=1, source_target_pairs={{0,2},{2,4},{4,6},{6,8},{8,10},{10,12},{12,14},{14,16},{16,18},{18... | collective-permute-start | bytes 92168 | tf_op jit(solution)/shard_map/ppermute | solution.py:19
  271.9 3.8 %collective-permute-start.19 = (f32[8,1024]{1,0:T(8,128)S(1)}, f32[8,1024]{1,0:T(8,128)S(1)}, u32[]{:S(2)}, u32[]{:S(2)}) collective-permute-start(f32[8,1024]{1,0:T(8,128)S(1)} %fusion.192), channel_id=1, source_target_pairs={{0,64},{32,96},{64,0},{96,32},{128,192},{160,224},{192,128},{224,1... | collective-permute-start | bytes 98312 | tf_op jit(solution)/shard_map/ppermute | solution.py:234
  275.7 6.8 %collective-permute-start.20 = (f32[8,1024]{1,0:T(8,128)S(1)}, f32[8,1024]{1,0:T(8,128)S(1)}, u32[]{:S(2)}, u32[]{:S(2)}) collective-permute-start(f32[8,1024]{1,0:T(8,128)S(1)} %add.537), channel_id=1, source_target_pairs={{0,128},{32,160},{64,192},{96,224},{128,0},{160,32},{192,64},{224,... | collective-permute-start | bytes 98312 | tf_op jit(solution)/shard_map/ppermute | solution.py:234
  282.4 14.8 %collective-permute-start.21 = (f32[8,1024]{1,0:T(8,128)S(1)}, f32[8,1024]{1,0:T(8,128)S(1)}, u32[]{:S(2)}, u32[]{:S(2)}) collective-permute-start(f32[8,1024]{1,0:T(8,128)S(1)} %get-tuple-element.43), channel_id=1, source_target_pairs={{0,1},{1,0},{2,3},{3,2},{4,5},{5,4},{6,7},{7,6},{8,9},{9,8},{10,11... | collective-permute-start | bytes 98312 | tf_op jit(solution)/shard_map/ppermute | solution.py:236
  288.5 57.7 %collective-permute-start.30 = (bf16[1024,1024]{1,0:T(8,128)(2,1)S(1)}, bf16[1024,1024]{1,0:T(8,128)(2,1)}, u32[]{:S(2)}, u32[]{:S(2)}) collective-permute-start(bf16[1024,1024]{1,0:T(8,128)(2,1)S(1)} %fusion.3), channel_id=1, source_target_pairs={{0,1},{1,0},{2,3},{3,2},{4,5},{5,4},{6,7},{7,6},{8,9},{9,8},{10,11... | collective-permute-start | bytes 6291464 | tf_op jit(solution)/shard_map/ppermute | solution.py:25
  291.9 6.5 %collective-permute-start.22 = (f32[8,1024]{1,0:T(8,128)S(1)}, f32[8,1024]{1,0:T(8,128)S(1)}, u32[]{:S(2)}, u32[]{:S(2)}) collective-permute-start(f32[8,1024]{1,0:T(8,128)S(1)} %get-tuple-element.43), channel_id=1, source_target_pairs={{0,2},{1,3},{2,0},{3,1},{4,6},{5,7},{6,4},{7,5},{8,10},{9,11},{10,... | collective-permute-start | bytes 98312 | tf_op jit(solution)/shard_map/ppermute | solution.py:236
  295.3 43.6 %collective-permute-start.23 = (f32[8,1024]{1,0:T(8,128)S(1)}, f32[8,1024]{1,0:T(8,128)S(1)}, u32[]{:S(2)}, u32[]{:S(2)}) collective-permute-start(f32[8,1024]{1,0:T(8,128)S(1)} %get-tuple-element.43), channel_id=1, source_target_pairs={{0,3},{1,2},{2,1},{3,0},{4,7},{5,6},{6,5},{7,4},{8,11},{9,10},{10,... | collective-permute-start | bytes 98312 | tf_op jit(solution)/shard_map/ppermute | solution.py:236
  297.3 41.6 %collective-permute-start.24 = (f32[8,1024]{1,0:T(8,128)S(1)}, f32[8,1024]{1,0:T(8,128)S(1)}, u32[]{:S(2)}, u32[]{:S(2)}) collective-permute-start(f32[8,1024]{1,0:T(8,128)S(1)} %get-tuple-element.43), channel_id=1, source_target_pairs={{0,4},{1,5},{2,6},{3,7},{4,0},{5,1},{6,2},{7,3},{8,12},{9,13},{10,... | collective-permute-start | bytes 98312 | tf_op jit(solution)/shard_map/ppermute | solution.py:236
  297.3 41.6 %collective-permute-start.25 = (f32[8,1024]{1,0:T(8,128)S(1)}, f32[8,1024]{1,0:T(8,128)S(1)}, u32[]{:S(2)}, u32[]{:S(2)}) collective-permute-start(f32[8,1024]{1,0:T(8,128)S(1)} %get-tuple-element.43), channel_id=1, source_target_pairs={{0,5},{1,4},{2,7},{3,6},{4,1},{5,0},{6,3},{7,2},{8,13},{9,12},{10,... | collective-permute-start | bytes 98312 | tf_op jit(solution)/shard_map/ppermute | solution.py:236
  298.5 40.5 %collective-permute-start.26 = (f32[8,1024]{1,0:T(8,128)S(1)}, f32[8,1024]{1,0:T(8,128)S(1)}, u32[]{:S(2)}, u32[]{:S(2)}) collective-permute-start(f32[8,1024]{1,0:T(8,128)S(1)} %get-tuple-element.43), channel_id=1, source_target_pairs={{0,6},{1,7},{2,4},{3,5},{4,2},{5,3},{6,0},{7,1},{8,14},{9,15},{10,... | collective-permute-start | bytes 98312 | tf_op jit(solution)/shard_map/ppermute | solution.py:236
  338.9 4.6 %collective-permute-start.27 = (f32[8,1024]{1,0:T(8,128)S(1)}, f32[8,1024]{1,0:T(8,128)S(1)}, u32[]{:S(2)}, u32[]{:S(2)}) collective-permute-start(f32[8,1024]{1,0:T(8,128)S(1)} %get-tuple-element.43), channel_id=1, source_target_pairs={{0,7},{1,6},{2,5},{3,4},{4,3},{5,2},{6,1},{7,0},{8,15},{9,14},{10,... | collective-permute-start | bytes 98312 | tf_op jit(solution)/shard_map/ppermute | solution.py:236
where the time goes:
time: 360 us; the launch traced here: 353 us
  waiting for transfers between devices  159 us (44%)
  starting transfers between devices  68.9 us (19%)
  other arithmetic  49.2 us (14%)
  local copies, waits for them, and re-layouts  43.4 us (12%)
  matrix products  30.5 us (8%)
    ppermute x7, waiting for transfers between devices, swap(): return lax.ppermute(value, axis, [(0, 1), (1, 0)])  45.6 us
    ppermute x7, waiting for transfers between devices, body(): lax.ppermute(chunk, local, [(i, i ^ offset) for i in range(8)])  43.8 us
    ppermute x7, waiting for transfers between devices, body(): lax.ppermute(piece, local, [(i, i ^ offset) for i in range(8)])  42 us
    all_to_all x1, waiting for transfers between devices, body(): totals = lax.all_to_all(back, GRP, split_axis=0, concat_axis=0, tiled=True)  13.7 us
    ppermute x7, starting transfers between devices, body(): lax.ppermute(piece, local, [(i, i ^ offset) for i in range(8)])  11.2 us
    all_to_all x1, starting transfers between devices, body(): lax.all_to_all(packed, GRP, split_axis=0, concat_axis=0, tiled=True)  10.9 us
    reduce_sum x1, other arithmetic, normalize(): square = jnp.mean(summed * summed, axis=-1, keepdims=True)  10.6 us
    ppermute x2, starting transfers between devices, padded_2(): after = lax.ppermute(initial, axis, down)  10.3 us
  transfers between devices with their start and end apart: 33, of which 12 were waited for; matrix products, arithmetic and copies ran while one was open for 21% of the time, Pallas kernels for 0%

commit v1 on v0

--- a/solution.py
+++ b/solution.py
@@ -145,10 +145,11 @@
     packed = jnp.dot(dispatch_table, both, preferred_element_type=jnp.float32).astype(jnp.bfloat16)
     packed = packed.reshape(expert_count, capacity, 2 * width)
     arrived = lax.all_to_all(packed, GRP, split_axis=0, concat_axis=0, tiled=True)
-    in_all = gather_slices(in_weights)
-    out_all = gather_slices(out_weights)
+    hid = in_weights.shape[1]
+    both_weights = gather_slices(jnp.stack([in_weights, out_weights.reshape(width, hid)]))
+    in_all = both_weights[:, :, 0]
+    out_all = both_weights[:, :, 1]
     slices = in_all.shape[0] * in_all.shape[1]
-    hid = in_weights.shape[1]
     in_all = in_all.reshape(slices, width, hid)
     out_all = out_all.reshape(slices, hid, width)
     flat = arrived.reshape(-1, 2 * width)
@@ -184,8 +185,11 @@
     in_term = in_term.reshape(2, 2, width, hid)
     out_term = out_term.reshape(2, 2, width, hid)
     terms = jnp.concatenate([in_term, out_term], axis=3).astype(jnp.bfloat16)
-    pair_terms = terms[0].astype(jnp.float32) + swap(terms[1], "c").astype(jnp.float32)
-    own_terms = pair_terms[0] + swap(pair_terms[1].astype(jnp.bfloat16), "xl").astype(jnp.float32)
+    terms = jnp.where(lax.axis_index("c") == 0, terms, terms[::-1])
+    terms = jnp.where(lax.axis_index("xl") == 0, terms, terms[:, ::-1])
+    terms = lax.psum_scatter(terms, "c", scatter_dimension=0, tiled=True)
+    terms = lax.psum_scatter(terms, "xl", scatter_dimension=1, tiled=True)
+    own_terms = terms.reshape(width, 2 * hid)
     mine = own_terms.astype(jnp.bfloat16)
     other = swap(mine, "dp")
     dp_first = lax.axis_index("dp") == 0

time: 360 us -> 423 us (1.18)
  local copies, waits for them, and re-layouts: 43.4 us -> 75 us
  other arithmetic: 49.2 us -> 69.3 us
  between operations: 1.86 us -> 15.9 us
  starting transfers between devices: 68.9 us -> 61.5 us
    ppermute x7 -> x3, waiting for transfers between devices: 45.6 us -> 0.01 us  [swap(): return lax.ppermute(value, axis, [(0, 1), (1, 0)])]
    ppermute x7, waiting for transfers between devices: 42 us -> 3.42 us  [body(): lax.ppermute(piece, local, [(i, i ^ offset) for i in range(8)])]
    ppermute x2, waiting for transfers between devices: 0.01 us -> 37.6 us  [padded_2(): after = lax.ppermute(initial, axis, down)]
    all_to_all x1, waiting for transfers between devices: 0.01 us -> 28.9 us  [body(): lax.all_to_all(packed, GRP, split_axis=0, concat_axis=0, tiled=True)]
    select_n x0 -> x2, other arithmetic: none -> 26.9 us  [the longest x1 13.5 us: body(): terms = jnp.where(lax.axis_index('c') == 0, terms, terms[::-1])]
    all_to_all x1, waiting for transfers between devices: 13.7 us -> 36.9 us  [body(): totals = lax.all_to_all(back, GRP, split_axis=0, concat_axis=0, tiled=True)]
    another operation x1 -> x5, local copies, waits for them, and re-layouts: 0.01 us -> 18.2 us  [the longest x1 7.63 us: body(): out_all = out_all.reshape(slices, hid, width)]
    reduce_sum x1, other arithmetic: 10.6 us -> 2.63 us  [normalize(): square = jnp.mean(summed * summed, axis=-1, keepdims=True)]
  transfers between devices with their start and end apart: 33 -> 31, of which waited for: 12 -> 11; matrix products, arithmetic and copies ran while one was open for 21% -> 19% of each run, Pallas kernels for 0% -> 0%
where the time goes in v1:
time: 423 us; the launch traced here: 416 us
  waiting for transfers between devices  163 us (39%)
  local copies, waits for them, and re-layouts  75 us (18%)
  other arithmetic  69.3 us (16%)
  starting transfers between devices  61.5 us (15%)
  matrix products  31.3 us (7%)
  between operations  15.9 us (4%)
    ppermute x7, waiting for transfers between devices, body(): lax.ppermute(chunk, local, [(i, i ^ offset) for i in range(8)])  40.1 us
    ppermute x2, waiting for transfers between devices, padded_2(): after = lax.ppermute(initial, axis, down)  37.6 us
    all_to_all x1, waiting for transfers between devices, body(): totals = lax.all_to_all(back, GRP, split_axis=0, concat_axis=0, tiled=True)  36.9 us
    all_to_all x1, waiting for transfers between devices, body(): lax.all_to_all(packed, GRP, split_axis=0, concat_axis=0, tiled=True)  28.9 us
    select_n x1, other arithmetic, body(): terms = jnp.where(lax.axis_index('c') == 0, terms, terms[::-1])  13.5 us
    select_n x1, other arithmetic, body(): terms = jnp.where(lax.axis_index('xl') == 0, terms, terms[:, ::-1])  13.5 us
    ppermute x7, starting transfers between devices, body(): lax.ppermute(piece, local, [(i, i ^ offset) for i in range(8)])  12 us
    ppermute x3, waiting for transfers between devices, body(): chunk = chunk + lax.ppermute(chunk, 'z', [(i, i ^ bit) for i in range(8)])  11.6 us
  transfers between devices with their start and end apart: 31, of which 11 were waited for; matrix products, arithmetic and copies ran while one was open for 19% of the time, Pallas kernels for 0%

profile of v1, /device:TPU:1, one launch (start us, length us, event | category | flops | bytes accessed | tf_op | source)
XLA Modules:
  0.0 415.6 jit_solution(16874821611767544353)
XLA Ops:
  7.2 1.3 constant_dynamic-update-slice_fusion.1
  8.6 2.2 stack_reshape_squeeze.3
  10.8 1.3 constant_dynamic-update-slice_fusion
  12.1 2.1 collective-permute-start.2
  14.2 3.1 collective-permute-start.1
  17.3 3.5 collective-permute-start
  23.2 37.6 %collective-permute-done.1 = bf16[15,1024]{1,0:T(8,128)(2,1)S(1)} collective-permute-done((bf16[15,1024]{1,0:T(8,128)(2,1)S(1)}, bf16[15,1024]{1,0:T(8,128)(2,1)S(1)}, u32[]{:S(2)}, u32[]{:S(2)}) %collective-permute-start.1) | collective-permute-done | bytes 30752 | tf_op jit(solution)/shard_map/ppermute | solution.py:20
  60.8 2.6 multiply_reduce_fusion.2
  64.6 4.8 %pad_maximum_fusion.2 = (bf16[2,2,1024,512]{3,2,1,0:T(8,128)(2,1)}, bf16[1,2,2,1024,512]{4,3,2,1,0:T(8,128)(2,1)}) fusion(bf16[1,2,1024,512]{3,2,1,0:T(8,128)(2,1)} %bitcast.42, bf16[1,2,1024,512]{3,2,1,0:T(8,128)(2,1)S(1)} %bitcast.259), kind=kLoop, calls=%fused_computation.10 | loop fusion | flops 2097152 | bytes 12582912 | tf_op jit(solution)/shard_map/stack | solution.py:29
  70.9 2.0 convolution_convert_fusion.2
  72.9 11.4 %all-to-all-start = ((bf16[32,16,2048]{2,1,0:T(8,128)(2,1)}), bf16[32,16,2048]{2,1,0:T(8,128)(2,1)S(1)}, u32[]{:S(2)}, u32[]{:S(2)}) async-start(bf16[32,16,2048]{2,1,0:T(8,128)(2,1)} %bitcast.39), calls=%async_computation | async-start | bytes 4194304 | tf_op jit(solution)/shard_map/all_to_all | solution.py:147
  84.6 5.8 %pad_maximum_fusion.1 = (bf16[2,2,1,1024,512]{4,3,2,1,0:T(8,128)(2,1)}, bf16[2,2,1,1024,512]{4,3,2,1,0:T(8,128)(2,1)}) fusion(bf16[1,2,2,1024,512]{4,3,2,1,0:T(8,128)(2,1)} %bitcast.44, bf16[1,2,2,1024,512]{4,3,2,1,0:T(8,128)(2,1)} %get-tuple-element.54), kind=kLoop, calls=%fused_computation.9 | loop fusion | flops 4194304 | bytes 16777216 | tf_op jit(solution)/shard_map/stack | solution.py:30
  90.4 6.3 %copy.47 = bf16[1024,4,512]{0,2,1:T(8,128)(2,1)} copy(bf16[1024,4,512]{2,0,1:T(8,128)(2,1)} %bitcast.251) | data formatting | bytes 8388608 | tf_op jit(solution)/shard_map/transpose | solution.py:160
  96.8 7.1 %reshape_reshape_squeeze.3 = bf16[2048,1024]{1,0:T(8,128)(2,1)} reshape(bf16[2,2,1,1024,512]{4,3,2,1,0:T(8,128)(2,1)} %get-tuple-element.49) | data formatting | bytes 8388608 | tf_op jit(solution)/shard_map/reshape;reshape;squeeze | solution.py:161
  103.9 28.9 %all-to-all-done = bf16[32,16,2048]{2,1,0:T(8,128)(2,1)S(1)} async-done(((bf16[32,16,2048]{2,1,0:T(8,128)(2,1)}), bf16[32,16,2048]{2,1,0:T(8,128)(2,1)S(1)}, u32[]{:S(2)}, u32[]{:S(2)}) %all-to-all-start) | async-done | bytes 2097184 | tf_op jit(solution)/shard_map/all_to_all | solution.py:147
  132.7 6.8 %multiply_convert_fusion.1 = (bf16[512,2048]{1,0:T(8,128)(2,1)S(1)}, f32[512,2048]{1,0:T(8,128)}) fusion(bf16[1024,2048]{0,1:T(8,128)(2,1)} %bitcast.260, bf16[512,2048]{1,0:T(8,128)(2,1)S(1)} %bitcast.263), kind=kOutput, calls=%fused_computation.13 | convolution fusion | flops 2152726528 | bytes 11534336 | tf_op jit(solution)/shard_map/dot_general | solution.py:162
  139.6 1.3 copy-done.78
  140.9 4.4 %convolution_convert_fusion = bf16[2048,1024]{1,0:T(8,128)(2,1)} fusion(bf16[512,2048]{1,0:T(8,128)(2,1)S(1)} %get-tuple-element.103, bf16[512,2048]{1,0:T(8,128)(2,1)S(1)} %bitcast.264), kind=kOutput, calls=%fused_computation.15 | convolution fusion | flops 2149580800 | bytes 7340032 | tf_op jit(solution)/shard_map/dot_general | solution.py:174
  145.3 7.1 %reshape.314 = bf16[2,2,1024,512]{3,2,1,0:T(8,128)(2,1)} reshape(bf16[2048,1024]{1,0:T(8,128)(2,1)} %convolution_convert_fusion) | data formatting | bytes 8388608 | tf_op jit(solution)/shard_map/reshape | solution.py:186
  152.4 5.9 %multiply_convert_fusion = bf16[512,2048]{1,0:T(8,128)(2,1)S(1)} fusion(f32[512,2048]{1,0:T(8,128)} %get-tuple-element.104, bf16[2048,1024]{1,0:T(8,128)(2,1)} %reshape_reshape_squeeze.3, bf16[512,2048]{1,0:T(8,128)(2,1)S(1)} %bitcast.265), kind=kOutput, calls=%fused_computation.12 | convolution fusion | flops 2156920832 | bytes 11534336 | tf_op jit(solution)/shard_map/dot_general | solution.py:172
  158.3 1.3 copy-done.80
  159.6 4.4 %convolution_convert_fusion.1 = bf16[1024,2048]{1,0:T(8,128)(2,1)} fusion(bf16[512,2048]{1,0:T(8,128)(2,1)S(1)} %multiply_convert_fusion, bf16[512,2048]{1,0:T(8,128)(2,1)S(1)} %bitcast.266), kind=kOutput, calls=%fused_computation.16 | convolution fusion | flops 2149580800 | bytes 7340032 | tf_op jit(solution)/shard_map/dot_general | solution.py:175
  163.9 8.0 %reshape.312 = bf16[1024,4,512]{2,1,0:T(4,128)(2,1)} reshape(bf16[1024,2048]{1,0:T(8,128)(2,1)} %convolution_convert_fusion.1) | data formatting | bytes 8388608 | tf_op jit(solution)/shard_map/reshape | solution.py:184
  172.0 5.0 %copy.52 = bf16[4,1024,512]{2,1,0:T(8,128)(2,1)} copy(bf16[4,1024,512]{2,0,1:T(4,128)(2,1)} %bitcast.250) | data formatting | bytes 8388608 | tf_op jit(solution)/shard_map/transpose | solution.py:184
  176.9 7.8 %pad_maximum_fusion = bf16[2,2,1024,1024]{3,2,1,0:T(8,128)(2,1)} fusion(bf16[2,2,1024,512]{3,2,1,0:T(8,128)(2,1)} %reshape.314, bf16[2,2,1024,512]{3,2,1,0:T(8,128)(2,1)} %bitcast.253), kind=kLoop, calls=%fused_computation.7 | loop fusion | flops 16777216 | bytes 16777216 | tf_op jit(solution)/shard_map/concatenate | solution.py:187
  184.7 13.5 %reverse_select_fusion.1 = bf16[2,2,1024,1024]{3,2,1,0:T(8,128)(2,1)} fusion(bf16[2,2,1024,1024]{3,2,1,0:T(8,128)(2,1)} %pad_maximum_fusion, pred[]{:T(512)S(6)} %eq.89), kind=kLoop, calls=%fused_computation.4 | loop fusion | flops 4194304 | bytes 16777216 | tf_op jit(solution)/shard_map/jit(_where)/select_n | solution.py:188
  198.2 13.5 %reverse_select_fusion = bf16[2,2,1024,1024]{3,2,1,0:T(8,128)(2,1)} fusion(bf16[2,2,1024,1024]{3,2,1,0:T(8,128)(2,1)} %reverse_select_fusion.1, pred[]{:T(512)S(6)} %eq.88), kind=kLoop, calls=%fused_computation.3 | loop fusion | flops 4194304 | bytes 16777216 | tf_op jit(solution)/shard_map/jit(_where)/select_n | solution.py:189
  211.7 7.6 %reshape_squeeze.11 = bf16[4,512,1024]{2,1,0:T(8,128)(2,1)} reshape(bf16[2,2,1,1024,512]{4,3,2,1,0:T(8,128)(2,1)} %get-tuple-element.49) | data formatting | bytes 8388608 | tf_op jit(solution)/shard_map/reshape;squeeze | solution.py:154
  219.4 4.7 %convolution_convert_fusion.3 = bf16[4,512,1024]{2,1,0:T(8,128)(2,1)S(1)} fusion(bf16[4,1024,512]{2,1,0:T(8,128)(2,1)} %bitcast.252, bf16[64,4,8,512]{3,2,1,0:T(8,128)(2,1)S(1)} %bitcast.373), kind=kOutput, calls=%fused_computation.18 | convolution fusion | flops 2149580800 | bytes 10485760 | tf_op jit(solution)/shard_map/rsh,sdh->srd/dot_general | solution.py:176
  225.0 1.8 copy-done.2
  226.8 2.3 convolution_convert_fusion.4
  230.0 1.6 pad_maximum_fusion.3
  231.6 7.3 %all-to-all-start.1 = ((bf16[32,16,2048]{2,1,0:T(8,128)(2,1)}), bf16[32,16,2048]{2,1,0:T(8,128)(2,1)S(1)}, u32[]{:S(2)}, u32[]{:S(2)}) async-start(bf16[32,16,2048]{2,1,0:T(8,128)(2,1)} %pad_maximum_fusion.3), calls=%async_computation.1 | async-start | bytes 4194304 | tf_op jit(solution)/shard_map/all_to_all | solution.py:204
  239.7 1.4 reduce_sum.361
  241.1 1.2 broadcast_multiply_fusion
  242.4 1.4 copy.50
  243.8 1.5 mul.1018
  245.3 1.5 copy.45
  248.7 1.2 compare_and_fusion.2
  249.9 36.9 %all-to-all-done.1 = bf16[32,16,2048]{2,1,0:T(8,128)(2,1)S(1)} async-done(((bf16[32,16,2048]{2,1,0:T(8,128)(2,1)}), bf16[32,16,2048]{2,1,0:T(8,128)(2,1)S(1)}, u32[]{:S(2)}, u32[]{:S(2)}) %all-to-all-start.1) | async-done | bytes 2097184 | tf_op jit(solution)/shard_map/all_to_all | solution.py:204
  286.8 2.5 gather_fusion
  289.2 1.9 gather.17
  291.2 1.3 fusion.9
  297.3 6.9 %collective-permute-start.12 = (f32[8,1024]{1,0:T(8,128)S(1)}, f32[8,1024]{1,0:T(8,128)S(1)}, u32[]{:S(2)}, u32[]{:S(2)}) collective-permute-start(f32[8,1024]{1,0:T(8,128)S(1)} %get-tuple-element.58), channel_id=1, source_target_pairs={{0,7},{1,6},{2,5},{3,4},{4,3},{5,2},{6,1},{7,0},{8,15},{9,14},{10,... | collective-permute-start | bytes 98312 | tf_op jit(solution)/shard_map/ppermute | solution.py:235
  305.2 2.9 collective-permute-start.8
  310.1 2.7 collective-permute-done.6
  312.8 2.5 collective-permute-start.15
  316.9 2.7 collective-permute-done.14
  320.4 1.1 collective-permute-start.16
  321.5 4.9 %collective-permute-start.5 = (bf16[15,1024]{1,0:T(8,128)(2,1)S(1)}, bf16[15,1024]{1,0:T(8,128)(2,1)S(1)}, u32[]{:S(2)}, u32[]{:S(2)}) collective-permute-start(bf16[15,1024]{1,0:T(8,128)(2,1)S(1)} %get-tuple-element.65), channel_id=1, source_target_pairs={{2,0},{4,2},{6,4},{8,6},{10,8},{12,10},{14,12},{16,14},{18,16},{20... | collective-permute-start | bytes 92168 | tf_op jit(solution)/shard_map/ppermute | solution.py:20
  326.4 2.8 collective-permute-start.4
  329.6 4.7 %collective-permute-done.17 = f32[8,1024]{1,0:T(8,128)S(1)} collective-permute-done((f32[8,1024]{1,0:T(8,128)S(1)}, f32[8,1024]{1,0:T(8,128)S(1)}, u32[]{:S(2)}, u32[]{:S(2)}) %collective-permute-start.17) | collective-permute-done | bytes 32800 | tf_op jit(solution)/shard_map/ppermute | solution.py:238
  334.7 6.9 %collective-permute-done.18 = f32[8,1024]{1,0:T(8,128)S(1)} collective-permute-done((f32[8,1024]{1,0:T(8,128)S(1)}, f32[8,1024]{1,0:T(8,128)S(1)}, u32[]{:S(2)}, u32[]{:S(2)}) %collective-permute-start.18) | collective-permute-done | bytes 32800 | tf_op jit(solution)/shard_map/ppermute | solution.py:238
  342.8 2.3 collective-permute-start.26
  345.4 2.8 fusion.148
  348.1 1.8 collective-permute-start.20
  351.3 1.8 collective-permute-start.23
  353.7 1.3 collective-permute-start.24
  355.7 38.0 %collective-permute-done.21 = f32[8,1024]{1,0:T(8,128)S(1)} collective-permute-done((f32[8,1024]{1,0:T(8,128)S(1)}, f32[8,1024]{1,0:T(8,128)S(1)}, u32[]{:S(2)}, u32[]{:S(2)}) %collective-permute-start.21) | collective-permute-done | bytes 32800 | tf_op jit(solution)/shard_map/ppermute | solution.py:240
  396.2 2.1 collective-permute-done.25
  398.9 1.5 gather_fusion.2
  402.5 2.5 convert_add_fusion
  405.0 1.9 fusion.174
  406.9 1.7 broadcast_in_dim_reshape.3
  (270 shorter events, 28.7 us)
Async XLA Ops:
  7.2 57.0 %copy-start = (bf16[1024,32]{0,1:T(8,128)(2,1)S(1)}, bf16[1024,32]{0,1:T(8,128)(2,1)}, u32[]{:S(2)}) copy-start(bf16[1024,32]{0,1:T(8,128)(2,1)} %param.11) | copy-start | bytes 196612
  7.2 56.8 %copy-start.6 = (f32[1024]{0:T(1024)S(1)}, f32[1024]{0:T(1024)}, u32[]{:S(2)}) copy-start(f32[1024]{0:T(1024)} %param.10) | copy-start | bytes 12292
  12.1 52.3 %collective-permute-start.2 = (bf16[2,1024,512]{2,1,0:T(8,128)(2,1)S(1)}, bf16[2,1024,512]{2,1,0:T(8,128)(2,1)}, u32[]{:S(2)}, u32[]{:S(2)}) collective-permute-start(bf16[2,1024,512]{2,1,0:T(8,128)(2,1)S(1)} %constant_dynamic-update-slice_fusion), channel_id=1, source_target_pairs={{0,4},{4,0},{1,5},{5,1},{2,6},{6,2},{3,7},{7,3},{8,12},{12,8},{9,1... | collective-permute-start | bytes 6291464 | tf_op jit(solution)/shard_map/ppermute | solution.py:25
  14.2 46.6 %collective-permute-start.1 = (bf16[15,1024]{1,0:T(8,128)(2,1)S(1)}, bf16[15,1024]{1,0:T(8,128)(2,1)S(1)}, u32[]{:S(2)}, u32[]{:S(2)}) collective-permute-start(bf16[15,1024]{1,0:T(8,128)(2,1)S(1)} %get-tuple-element.69), channel_id=1, source_target_pairs={{2,0},{4,2},{6,4},{8,6},{10,8},{12,10},{14,12},{16,14},{18,16},{20... | collective-permute-start | bytes 92168 | tf_op jit(solution)/shard_map/ppermute | solution.py:20
  17.3 43.5 %collective-permute-start = (bf16[15,1024]{1,0:T(8,128)(2,1)S(1)}, bf16[15,1024]{1,0:T(8,128)(2,1)S(1)}, u32[]{:S(2)}, u32[]{:S(2)}) collective-permute-start(bf16[15,1024]{1,0:T(8,128)(2,1)S(1)} %get-tuple-element.68), channel_id=1, source_target_pairs={{0,2},{2,4},{4,6},{6,8},{8,10},{10,12},{12,14},{14,16},{16,18},{18... | collective-permute-start | bytes 92168 | tf_op jit(solution)/shard_map/ppermute | solution.py:19
  21.3 42.2 %copy-start.7 = (f32[1,1024]{1,0:T(1,128)}, f32[1,1024]{1,0:T(1,128)S(1)}, u32[]{:S(2)}) copy-start(f32[1,1024]{1,0:T(1,128)S(1)} %get-tuple-element.92) | copy-start | bytes 12292
  21.3 42.2 %copy-start.9 = (f32[1,1024]{1,0:T(1,128)}, f32[1,1024]{1,0:T(1,128)S(1)}, u32[]{:S(2)}) copy-start(f32[1,1024]{1,0:T(1,128)S(1)} %get-tuple-element.93) | copy-start | bytes 12292
  69.4 15.2 %collective-permute-start.3 = (bf16[2,2,1024,512]{3,2,1,0:T(8,128)(2,1)}, bf16[2,2,1024,512]{3,2,1,0:T(8,128)(2,1)}, u32[]{:S(2)}, u32[]{:S(2)}) collective-permute-start(bf16[2,2,1024,512]{3,2,1,0:T(8,128)(2,1)} %get-tuple-element.53), channel_id=1, source_target_pairs={{0,2},{2,0},{1,3},{3,1},{4,6},{6,4},{5,7},{7,5},{8,10},{10,8},{9,1... | collective-permute-start | bytes 12582920 | tf_op jit(solution)/shard_map/ppermute | solution.py:25
  72.9 59.8 %all-to-all-start = ((bf16[32,16,2048]{2,1,0:T(8,128)(2,1)}), bf16[32,16,2048]{2,1,0:T(8,128)(2,1)S(1)}, u32[]{:S(2)}, u32[]{:S(2)}) async-start(bf16[32,16,2048]{2,1,0:T(8,128)(2,1)} %bitcast.39), calls=%async_computation | async-start | bytes 4194304 | tf_op jit(solution)/shard_map/all_to_all | solution.py:147
  84.4 154.6 %reduce-scatter.3.cloned.1.call-start = ((), (), s32[]{:S(2)}) async-start(), calls=%async_computation.4 | async-start | bytes 12582912 | tf_op jit(solution)/shard_map/reduce_scatter | solution.py:190
  231.6 55.2 %all-to-all-start.1 = ((bf16[32,16,2048]{2,1,0:T(8,128)(2,1)}), bf16[32,16,2048]{2,1,0:T(8,128)(2,1)S(1)}, u32[]{:S(2)}, u32[]{:S(2)}) async-start(bf16[32,16,2048]{2,1,0:T(8,128)(2,1)} %pad_maximum_fusion.3), calls=%async_computation.1 | async-start | bytes 4194304 | tf_op jit(solution)/shard_map/all_to_all | solution.py:204
  238.9 103.9 %reduce-scatter.5.cloned.1.call-start = ((), (), s32[]{:S(2)}) async-start(), calls=%async_computation.5 | async-start | bytes 6291456 | tf_op jit(solution)/shard_map/reduce_scatter | solution.py:191
  295.0 50.1 %copy-start.8 = (f32[1,1024]{1,0:T(1,128)S(1)}, f32[1,1024]{1,0:T(1,128)}, u32[]{:S(2)}) copy-start(f32[1,1024]{1,0:T(1,128)} %copy-done.7) | copy-start | bytes 12292
  295.0 50.1 %copy-start.10 = (f32[1,1024]{1,0:T(1,128)S(1)}, f32[1,1024]{1,0:T(1,128)}, u32[]{:S(2)}) copy-start(f32[1,1024]{1,0:T(1,128)} %copy-done.9) | copy-start | bytes 12292
  295.0 50.1 %copy-start.12 = (f32[1,1024]{1,0:T(1,128)S(1)}, f32[1,1024]{1,0:T(1,128)}, u32[]{:S(2)}) copy-start(f32[1,1024]{1,0:T(1,128)} %copy-done.11) | copy-start | bytes 12292
  295.1 50.1 %copy-start.14 = (f32[1,1024]{1,0:T(1,128)S(1)}, f32[1,1024]{1,0:T(1,128)}, u32[]{:S(2)}) copy-start(f32[1,1024]{1,0:T(1,128)} %copy-done.13) | copy-start | bytes 12292
  295.1 50.1 %copy-start.16 = (f32[1,1024]{1,0:T(1,128)S(1)}, f32[1,1024]{1,0:T(1,128)}, u32[]{:S(2)}) copy-start(f32[1,1024]{1,0:T(1,128)} %copy-done.15) | copy-start | bytes 12292
  295.1 50.1 %copy-start.18 = (f32[1,1024]{1,0:T(1,128)S(1)}, f32[1,1024]{1,0:T(1,128)}, u32[]{:S(2)}) copy-start(f32[1,1024]{1,0:T(1,128)} %copy-done.17) | copy-start | bytes 12292
  295.1 50.1 %copy-start.20 = (f32[1,1024]{1,0:T(1,128)S(1)}, f32[1,1024]{1,0:T(1,128)}, u32[]{:S(2)}) copy-start(f32[1,1024]{1,0:T(1,128)} %copy-done.19) | copy-start | bytes 12292
  295.1 50.1 %copy-start.22 = (f32[1,1024]{1,0:T(1,128)S(1)}, f32[1,1024]{1,0:T(1,128)}, u32[]{:S(2)}) copy-start(f32[1,1024]{1,0:T(1,128)} %copy-done.21) | copy-start | bytes 12292
  295.1 50.1 %copy-start.24 = (f32[1,1024]{1,0:T(1,128)S(1)}, f32[1,1024]{1,0:T(1,128)}, u32[]{:S(2)}) copy-start(f32[1,1024]{1,0:T(1,128)} %copy-done.23) | copy-start | bytes 12292
  295.1 50.1 %copy-start.26 = (f32[1,1024]{1,0:T(1,128)S(1)}, f32[1,1024]{1,0:T(1,128)}, u32[]{:S(2)}) copy-start(f32[1,1024]{1,0:T(1,128)} %copy-done.25) | copy-start | bytes 12292
  295.1 50.1 %copy-start.28 = (f32[1,1024]{1,0:T(1,128)S(1)}, f32[1,1024]{1,0:T(1,128)}, u32[]{:S(2)}) copy-start(f32[1,1024]{1,0:T(1,128)} %copy-done.27) | copy-start | bytes 12292
  295.1 50.1 %copy-start.30 = (f32[1,1024]{1,0:T(1,128)S(1)}, f32[1,1024]{1,0:T(1,128)}, u32[]{:S(2)}) copy-start(f32[1,1024]{1,0:T(1,128)} %copy-done.29) | copy-start | bytes 12292
  295.1 50.1 %copy-start.32 = (f32[1,1024]{1,0:T(1,128)S(1)}, f32[1,1024]{1,0:T(1,128)}, u32[]{:S(2)}) copy-start(f32[1,1024]{1,0:T(1,128)} %copy-done.31) | copy-start | bytes 12292
  295.2 50.1 %copy-start.34 = (f32[1,1024]{1,0:T(1,128)S(1)}, f32[1,1024]{1,0:T(1,128)}, u32[]{:S(2)}) copy-start(f32[1,1024]{1,0:T(1,128)} %copy-done.33) | copy-start | bytes 12292
  295.2 50.1 %copy-start.36 = (f32[1,1024]{1,0:T(1,128)S(1)}, f32[1,1024]{1,0:T(1,128)}, u32[]{:S(2)}) copy-start(f32[1,1024]{1,0:T(1,128)} %copy-done.35) | copy-start | bytes 12292
  295.2 50.1 %copy-start.38 = (f32[1,1024]{1,0:T(1,128)S(1)}, f32[1,1024]{1,0:T(1,128)}, u32[]{:S(2)}) copy-start(f32[1,1024]{1,0:T(1,128)} %copy-done.37) | copy-start | bytes 12292
  295.2 50.1 %copy-start.40 = (f32[1,1024]{1,0:T(1,128)S(1)}, f32[1,1024]{1,0:T(1,128)}, u32[]{:S(2)}) copy-start(f32[1,1024]{1,0:T(1,128)} %copy-done.39) | copy-start | bytes 12292
  295.2 50.1 %copy-start.42 = (f32[1,1024]{1,0:T(1,128)S(1)}, f32[1,1024]{1,0:T(1,128)}, u32[]{:S(2)}) copy-start(f32[1,1024]{1,0:T(1,128)} %copy-done.41) | copy-start | bytes 12292
  295.2 50.1 %copy-start.44 = (f32[1,1024]{1,0:T(1,128)S(1)}, f32[1,1024]{1,0:T(1,128)}, u32[]{:S(2)}) copy-start(f32[1,1024]{1,0:T(1,128)} %copy-done.43) | copy-start | bytes 12292
  295.2 50.1 %copy-start.46 = (f32[1,1024]{1,0:T(1,128)S(1)}, f32[1,1024]{1,0:T(1,128)}, u32[]{:S(2)}) copy-start(f32[1,1024]{1,0:T(1,128)} %copy-done.45) | copy-start | bytes 12292
  295.2 50.1 %copy-start.48 = (f32[1,1024]{1,0:T(1,128)S(1)}, f32[1,1024]{1,0:T(1,128)}, u32[]{:S(2)}) copy-start(f32[1,1024]{1,0:T(1,128)} %copy-done.47) | copy-start | bytes 12292
  295.2 50.1 %copy-start.50 = (f32[1,1024]{1,0:T(1,128)S(1)}, f32[1,1024]{1,0:T(1,128)}, u32[]{:S(2)}) copy-start(f32[1,1024]{1,0:T(1,128)} %copy-done.49) | copy-start | bytes 12292
  295.2 50.1 %copy-start.52 = (f32[1,1024]{1,0:T(1,128)S(1)}, f32[1,1024]{1,0:T(1,128)}, u32[]{:S(2)}) copy-start(f32[1,1024]{1,0:T(1,128)} %copy-done.51) | copy-start | bytes 12292
  295.3 50.1 %copy-start.54 = (f32[1,1024]{1,0:T(1,128)S(1)}, f32[1,1024]{1,0:T(1,128)}, u32[]{:S(2)}) copy-start(f32[1,1024]{1,0:T(1,128)} %copy-done.53) | copy-start | bytes 12292
  295.3 50.1 %copy-start.56 = (f32[1,1024]{1,0:T(1,128)S(1)}, f32[1,1024]{1,0:T(1,128)}, u32[]{:S(2)}) copy-start(f32[1,1024]{1,0:T(1,128)} %copy-done.55) | copy-start | bytes 12292
  295.3 50.1 %copy-start.58 = (f32[1,1024]{1,0:T(1,128)S(1)}, f32[1,1024]{1,0:T(1,128)}, u32[]{:S(2)}) copy-start(f32[1,1024]{1,0:T(1,128)} %copy-done.57) | copy-start | bytes 12292
  295.3 50.1 %copy-start.60 = (f32[1,1024]{1,0:T(1,128)S(1)}, f32[1,1024]{1,0:T(1,128)}, u32[]{:S(2)}) copy-start(f32[1,1024]{1,0:T(1,128)} %copy-done.59) | copy-start | bytes 12292
  295.3 50.1 %copy-start.62 = (f32[1,1024]{1,0:T(1,128)S(1)}, f32[1,1024]{1,0:T(1,128)}, u32[]{:S(2)}) copy-start(f32[1,1024]{1,0:T(1,128)} %copy-done.61) | copy-start | bytes 12292
  297.3 10.7 %collective-permute-start.12 = (f32[8,1024]{1,0:T(8,128)S(1)}, f32[8,1024]{1,0:T(8,128)S(1)}, u32[]{:S(2)}, u32[]{:S(2)}) collective-permute-start(f32[8,1024]{1,0:T(8,128)S(1)} %get-tuple-element.58), channel_id=1, source_target_pairs={{0,7},{1,6},{2,5},{3,4},{4,3},{5,2},{6,1},{7,0},{8,15},{9,14},{10,... | collective-permute-start | bytes 98312 | tf_op jit(solution)/shard_map/ppermute | solution.py:235
  304.2 4.4 %collective-permute-start.11 = (f32[8,1024]{1,0:T(8,128)S(1)}, f32[8,1024]{1,0:T(8,128)S(1)}, u32[]{:S(2)}, u32[]{:S(2)}) collective-permute-start(f32[8,1024]{1,0:T(8,128)S(1)} %get-tuple-element.59), channel_id=1, source_target_pairs={{0,6},{1,7},{2,4},{3,5},{4,2},{5,3},{6,0},{7,1},{8,14},{9,15},{10,... | collective-permute-start | bytes 98312 | tf_op jit(solution)/shard_map/ppermute | solution.py:235
  304.2 5.2 %collective-permute-start.10 = (f32[8,1024]{1,0:T(8,128)S(1)}, f32[8,1024]{1,0:T(8,128)S(1)}, u32[]{:S(2)}, u32[]{:S(2)}) collective-permute-start(f32[8,1024]{1,0:T(8,128)S(1)} %get-tuple-element.60), channel_id=1, source_target_pairs={{0,5},{1,4},{2,7},{3,6},{4,1},{5,0},{6,3},{7,2},{8,13},{9,12},{10,... | collective-permute-start | bytes 98312 | tf_op jit(solution)/shard_map/ppermute | solution.py:235
  304.3 5.1 %collective-permute-start.9 = (f32[8,1024]{1,0:T(8,128)S(1)}, f32[8,1024]{1,0:T(8,128)S(1)}, u32[]{:S(2)}, u32[]{:S(2)}) collective-permute-start(f32[8,1024]{1,0:T(8,128)S(1)} %get-tuple-element.61), channel_id=1, source_target_pairs={{0,4},{1,5},{2,6},{3,7},{4,0},{5,1},{6,2},{7,3},{8,12},{9,13},{10,... | collective-permute-start | bytes 98312 | tf_op jit(solution)/shard_map/ppermute | solution.py:235
  305.2 5.0 %collective-permute-start.8 = (f32[8,1024]{1,0:T(8,128)S(1)}, f32[8,1024]{1,0:T(8,128)S(1)}, u32[]{:S(2)}, u32[]{:S(2)}) collective-permute-start(f32[8,1024]{1,0:T(8,128)S(1)} %get-tuple-element.62), channel_id=1, source_target_pairs={{0,3},{1,2},{2,1},{3,0},{4,7},{5,6},{6,5},{7,4},{8,11},{9,10},{10,... | collective-permute-start | bytes 98312 | tf_op jit(solution)/shard_map/ppermute | solution.py:235
  308.0 2.1 collective-permute-start.7
  308.5 4.3 %collective-permute-start.6 = (f32[8,1024]{1,0:T(8,128)S(1)}, f32[8,1024]{1,0:T(8,128)S(1)}, u32[]{:S(2)}, u32[]{:S(2)}) collective-permute-start(f32[8,1024]{1,0:T(8,128)S(1)} %get-tuple-element.57), channel_id=1, source_target_pairs={{0,1},{1,0},{2,3},{3,2},{4,5},{5,4},{6,7},{7,6},{8,9},{9,8},{10,11... | collective-permute-start | bytes 98312 | tf_op jit(solution)/shard_map/ppermute | solution.py:235
  312.8 4.1 collective-permute-start.15
  315.3 4.3 %collective-permute-start.14 = (f32[8,1024]{1,0:T(8,128)S(1)}, f32[8,1024]{1,0:T(8,128)S(1)}, u32[]{:S(2)}, u32[]{:S(2)}) collective-permute-start(f32[8,1024]{1,0:T(8,128)S(1)} %fusion.159), channel_id=1, source_target_pairs={{0,16},{8,24},{16,0},{24,8},{1,17},{9,25},{17,1},{25,9},{2,18},{10... | collective-permute-start | bytes 98312 | tf_op jit(solution)/shard_map/ppermute | solution.py:35
  315.7 3.9 collective-permute-start.13
  320.4 8.8 %collective-permute-start.16 = (f32[8,1024]{1,0:T(8,128)S(1)}, f32[8,1024]{1,0:T(8,128)S(1)}, u32[]{:S(2)}, u32[]{:S(2)}) collective-permute-start(f32[8,1024]{1,0:T(8,128)S(1)} %fusion.153), channel_id=1, source_target_pairs={{0,32},{32,0},{64,96},{96,64},{128,160},{160,128},{192,224},{224,1... | collective-permute-start | bytes 98312 | tf_op jit(solution)/shard_map/ppermute | solution.py:238
  321.5 13.0 %collective-permute-start.5 = (bf16[15,1024]{1,0:T(8,128)(2,1)S(1)}, bf16[15,1024]{1,0:T(8,128)(2,1)S(1)}, u32[]{:S(2)}, u32[]{:S(2)}) collective-permute-start(bf16[15,1024]{1,0:T(8,128)(2,1)S(1)} %get-tuple-element.65), channel_id=1, source_target_pairs={{2,0},{4,2},{6,4},{8,6},{10,8},{12,10},{14,12},{16,14},{18,16},{20... | collective-permute-start | bytes 92168 | tf_op jit(solution)/shard_map/ppermute | solution.py:20
  326.4 8.2 %collective-permute-start.4 = (bf16[15,1024]{1,0:T(8,128)(2,1)S(1)}, bf16[15,1024]{1,0:T(8,128)(2,1)S(1)}, u32[]{:S(2)}, u32[]{:S(2)}) collective-permute-start(bf16[15,1024]{1,0:T(8,128)(2,1)S(1)} %get-tuple-element.64), channel_id=1, source_target_pairs={{0,2},{2,4},{4,6},{6,8},{8,10},{10,12},{12,14},{14,16},{16,18},{18... | collective-permute-start | bytes 92168 | tf_op jit(solution)/shard_map/ppermute | solution.py:19
  329.3 5.1 %collective-permute-start.17 = (f32[8,1024]{1,0:T(8,128)S(1)}, f32[8,1024]{1,0:T(8,128)S(1)}, u32[]{:S(2)}, u32[]{:S(2)}) collective-permute-start(f32[8,1024]{1,0:T(8,128)S(1)} %fusion.186), channel_id=1, source_target_pairs={{0,64},{32,96},{64,0},{96,32},{128,192},{160,224},{192,128},{224,1... | collective-permute-start | bytes 98312 | tf_op jit(solution)/shard_map/ppermute | solution.py:238
  334.3 7.2 %collective-permute-start.18 = (f32[8,1024]{1,0:T(8,128)S(1)}, f32[8,1024]{1,0:T(8,128)S(1)}, u32[]{:S(2)}, u32[]{:S(2)}) collective-permute-start(f32[8,1024]{1,0:T(8,128)S(1)} %add.535), channel_id=1, source_target_pairs={{0,128},{32,160},{64,192},{96,224},{128,0},{160,32},{192,64},{224,... | collective-permute-start | bytes 98312 | tf_op jit(solution)/shard_map/ppermute | solution.py:238
  342.2 9.2 %collective-permute-start.19 = (f32[8,1024]{1,0:T(8,128)S(1)}, f32[8,1024]{1,0:T(8,128)S(1)}, u32[]{:S(2)}, u32[]{:S(2)}) collective-permute-start(f32[8,1024]{1,0:T(8,128)S(1)} %get-tuple-element.43), channel_id=1, source_target_pairs={{0,1},{1,0},{2,3},{3,2},{4,5},{5,4},{6,7},{7,6},{8,9},{9,8},{10,11... | collective-permute-start | bytes 98312 | tf_op jit(solution)/shard_map/ppermute | solution.py:240
  342.8 59.7 %copy-start.4 = (bf16[1,1,1024,1024]{3,2,1,0:T(8,128)(2,1)S(1)}, bf16[1,1,1024,1024]{3,2,1,0:T(8,128)(2,1)}, u32[]{:S(2)}) copy-start(bf16[1,1,1024,1024]{3,2,1,0:T(8,128)(2,1)} %reduce-scatter.5.cloned.1.call-done) | copy-start | bytes 6291460
  342.8 59.7 %collective-permute-start.26 = (bf16[1024,1024]{1,0:T(8,128)(2,1)}, bf16[1024,1024]{1,0:T(8,128)(2,1)}, u32[]{:S(2)}, u32[]{:S(2)}) collective-permute-start(bf16[1024,1024]{1,0:T(8,128)(2,1)} %bitcast.267), channel_id=1, source_target_pairs={{0,1},{1,0},{2,3},{3,2},{4,5},{5,4},{6,7},{7,6},{8,9},{9,8},{10,11... | collective-permute-start | bytes 6291464 | tf_op jit(solution)/shard_map/ppermute | solution.py:25
  348.1 5.6 %collective-permute-start.20 = (f32[8,1024]{1,0:T(8,128)S(1)}, f32[8,1024]{1,0:T(8,128)S(1)}, u32[]{:S(2)}, u32[]{:S(2)}) collective-permute-start(f32[8,1024]{1,0:T(8,128)S(1)} %get-tuple-element.43), channel_id=1, source_target_pairs={{0,2},{1,3},{2,0},{3,1},{4,6},{5,7},{6,4},{7,5},{8,10},{9,11},{10,... | collective-permute-start | bytes 98312 | tf_op jit(solution)/shard_map/ppermute | solution.py:240
  350.0 43.8 %collective-permute-start.21 = (f32[8,1024]{1,0:T(8,128)S(1)}, f32[8,1024]{1,0:T(8,128)S(1)}, u32[]{:S(2)}, u32[]{:S(2)}) collective-permute-start(f32[8,1024]{1,0:T(8,128)S(1)} %get-tuple-element.43), channel_id=1, source_target_pairs={{0,3},{1,2},{2,1},{3,0},{4,7},{5,6},{6,5},{7,4},{8,11},{9,10},{10,... | collective-permute-start | bytes 98312 | tf_op jit(solution)/shard_map/ppermute | solution.py:240
  350.8 43.6 %collective-permute-start.22 = (f32[8,1024]{1,0:T(8,128)S(1)}, f32[8,1024]{1,0:T(8,128)S(1)}, u32[]{:S(2)}, u32[]{:S(2)}) collective-permute-start(f32[8,1024]{1,0:T(8,128)S(1)} %get-tuple-element.43), channel_id=1, source_target_pairs={{0,4},{1,5},{2,6},{3,7},{4,0},{5,1},{6,2},{7,3},{8,12},{9,13},{10,... | collective-permute-start | bytes 98312 | tf_op jit(solution)/shard_map/ppermute | solution.py:240
  351.3 43.6 %collective-permute-start.23 = (f32[8,1024]{1,0:T(8,128)S(1)}, f32[8,1024]{1,0:T(8,128)S(1)}, u32[]{:S(2)}, u32[]{:S(2)}) collective-permute-start(f32[8,1024]{1,0:T(8,128)S(1)} %get-tuple-element.43), channel_id=1, source_target_pairs={{0,5},{1,4},{2,7},{3,6},{4,1},{5,0},{6,3},{7,2},{8,13},{9,12},{10,... | collective-permute-start | bytes 98312 | tf_op jit(solution)/shard_map/ppermute | solution.py:240
  353.7 41.9 %collective-permute-start.24 = (f32[8,1024]{1,0:T(8,128)S(1)}, f32[8,1024]{1,0:T(8,128)S(1)}, u32[]{:S(2)}, u32[]{:S(2)}) collective-permute-start(f32[8,1024]{1,0:T(8,128)S(1)} %get-tuple-element.43), channel_id=1, source_target_pairs={{0,6},{1,7},{2,4},{3,5},{4,2},{5,3},{6,0},{7,1},{8,14},{9,15},{10,... | collective-permute-start | bytes 98312 | tf_op jit(solution)/shard_map/ppermute | solution.py:240
  393.7 4.6 %collective-permute-start.25 = (f32[8,1024]{1,0:T(8,128)S(1)}, f32[8,1024]{1,0:T(8,128)S(1)}, u32[]{:S(2)}, u32[]{:S(2)}) collective-permute-start(f32[8,1024]{1,0:T(8,128)S(1)} %get-tuple-element.43), channel_id=1, source_target_pairs={{0,7},{1,6},{2,5},{3,4},{4,3},{5,2},{6,1},{7,0},{8,15},{9,14},{10,... | collective-permute-start | bytes 98312 | tf_op jit(solution)/shard_map/ppermute | solution.py:240
  (49 other events, 1283.0 us)
Sparse Core Ops, SparseCore 0:
  211.8 22.3 reduce-scatter.2
  242.3 62.3 reduce-scatter.4
